TPU v7x, 256 devices: a whole 4x4x8 slice. The times are simulated.
256 devices in a mesh: pipe: 8 (over y, core), ctx: 32 (over x, z).
Axes of the slice: x: 4, y: 4, z: 8, core: 2. Of those that a mesh axis runs over, the one named last changes fastest.
Arguments:
- queries: bfloat16 [8, 4096, 4096], P('pipe', 'ctx'), may hold values from -240 to 240
- keys: bfloat16 [8, 4096, 4096], P('pipe', 'ctx'), may hold values from -6 to 6
- values: bfloat16 [8, 4096, 4096], P('pipe', 'ctx'), may hold values from -6 to 6
- attn_out: bfloat16 [8, 4096, 4096], P('pipe', 'ctx'), may hold values from -3 to 3
- out_grad: bfloat16 [8, 4096, 4096], P('pipe', 'ctx'), may hold values from -24 to 24
- random_blocks: int32 [8, 32, 64, 3], P('pipe', 'ctx'), may hold values from 0 to 63
- global_blocks: int32 [8, 2], P('pipe'), may hold values from 0 to 63, as said below
- radius: int32 [8, 32], P('pipe', 'ctx'), may hold values from 1 to 2, as said below
Outputs:
- grad_queries: bfloat16 [8, 4096, 4096], P('pipe', 'ctx')
- grad_keys: bfloat16 [8, 4096, 4096], P('pipe', 'ctx')
- grad_values: bfloat16 [8, 4096, 4096], P('pipe', 'ctx')
Inputs may be any that keep to these rules, and one draw needn't show every extreme that they name: `global_blocks`: the 2 entries of a section differ. In every section some head has radius 2 and some head has radius 1.
All inputs are finite; a program needn't handle non-finite values.
Results may differ from a plain program's by a relative error of at most 0.0049.
Values may be sent and summed in bfloat16 or wider, within the bound.
No kernel may reach another device: no remote copies, remote signals or barrier semaphores. Data moves between devices by JAX's collectives and lax.ppermute only.
A program may use at most 64 MiB of HBM per device.

v0:
```python
import jax
import jax.numpy as jnp
from jax import lax
from jax.sharding import PartitionSpec as P

HD = 128
BLK = 64
RMAX = 2
NR = 3
QG = 8
KB = 10


def passed_along(value, axis, steps):
    count = lax.axis_size(axis)
    pairs = [(source, (source + steps) % count) for source in range(count)]
    return lax.ppermute(value, axis, pairs)


def slot_table(random_list, global_list, head_radius, block_count):
    blocks = jnp.arange(block_count, dtype=jnp.int32)[:, None]
    offsets = jnp.arange(-RMAX, RMAX + 1, dtype=jnp.int32)[None, :]
    window = blocks + offsets
    window_ok = (jnp.abs(offsets) <= head_radius) & (window >= 0) & (window < block_count)
    window = jnp.clip(window, 0, block_count - 1)
    global_slots = jnp.broadcast_to(global_list[None, :], (block_count, global_list.shape[0]))
    global_ok = jnp.abs(global_slots - blocks) > head_radius
    random_ok = jnp.abs(random_list - blocks) > head_radius
    random_ok = random_ok & jnp.all(random_list[:, :, None] != global_list[None, None, :], axis=2)
    earlier = jnp.arange(NR)[None, :] < jnp.arange(NR)[:, None]
    repeated = jnp.any((random_list[:, :, None] == random_list[:, None, :]) & earlier[None], axis=2)
    random_ok = random_ok & jnp.logical_not(repeated)
    slot_index = jnp.concatenate([window, global_slots, random_list], axis=1)
    slot_valid = jnp.concatenate([window_ok, global_ok, random_ok], axis=1)
    return (slot_index, slot_valid)


def lane_sums(first, second):
    product = first.astype(jnp.float32) * second.astype(jnp.float32)
    flat = product.reshape(-1, product.shape[-1])
    ones_column = jnp.ones((product.shape[-1],), jnp.float32)
    summed = jnp.dot(
        flat, ones_column, precision=lax.Precision.HIGHEST, preferred_element_type=jnp.float32
    )
    return summed.reshape(product.shape[:-1])


def head_grads(
    query_rows,
    key_rows,
    value_rows,
    grad_rows,
    correction_rows,
    random_list,
    global_list,
    head_radius,
):
    block_count = query_rows.shape[0] // BLK
    score_scale = HD ** (-0.5)
    slot_index, slot_valid = slot_table(random_list, global_list, head_radius, block_count)
    query_blocks = query_rows.reshape(block_count, BLK, HD)
    key_blocks = key_rows.reshape(block_count, BLK, HD)
    value_blocks = value_rows.reshape(block_count, BLK, HD)
    grad_blocks = grad_rows.reshape(block_count, BLK, HD)
    correction = correction_rows.reshape(block_count, BLK)
    block_ids = jnp.arange(block_count, dtype=jnp.int32)[:, None]

    def one_group(totals, first_block):
        key_total, value_total = totals
        group_index = lax.dynamic_slice_in_dim(slot_index, first_block, QG, 0)
        group_valid = lax.dynamic_slice_in_dim(slot_valid, first_block, QG, 0)
        group_query = lax.dynamic_slice_in_dim(query_blocks, first_block, QG, 0)
        group_grad = lax.dynamic_slice_in_dim(grad_blocks, first_block, QG, 0)
        group_corr = lax.dynamic_slice_in_dim(correction, first_block, QG, 0)
        key_tiles = key_blocks[group_index].reshape(QG, KB * BLK, HD)
        value_tiles = value_blocks[group_index].reshape(QG, KB * BLK, HD)
        key_live = jnp.repeat(group_valid, BLK, axis=1)
        scores = (
            jnp.einsum("bid,bjd->bij", group_query, key_tiles, preferred_element_type=jnp.float32)
            * score_scale
        )
        scores = jnp.where(key_live[:, None, :], scores, -jnp.inf)
        row_max = jnp.max(scores, axis=-1, keepdims=True)
        weights = jnp.exp(scores - row_max)
        attention = weights / jnp.sum(weights, axis=-1, keepdims=True)
        attention_low = attention.astype(jnp.bfloat16)
        dprobs = jnp.einsum(
            "bid,bjd->bij", group_grad, value_tiles, preferred_element_type=jnp.float32
        )
        dscores_low = (attention * (dprobs - group_corr[:, :, None])).astype(jnp.bfloat16)
        query_grad = (
            jnp.einsum("bij,bjd->bid", dscores_low, key_tiles, preferred_element_type=jnp.float32)
            * score_scale
        ).astype(jnp.bfloat16)
        key_part = jnp.einsum(
            "bij,bid->bjd", dscores_low, group_query, preferred_element_type=jnp.float32
        ).reshape(QG * KB, BLK * HD)
        value_part = jnp.einsum(
            "bij,bid->bjd", attention_low, group_grad, preferred_element_type=jnp.float32
        ).reshape(QG * KB, BLK * HD)
        flat_index = group_index.reshape(1, -1)
        placing = (block_ids == flat_index).astype(jnp.float32)
        key_total = key_total + jnp.dot(
            placing, key_part, precision=lax.Precision.HIGHEST, preferred_element_type=jnp.float32
        )
        value_total = value_total + jnp.dot(
            placing, value_part, precision=lax.Precision.HIGHEST, preferred_element_type=jnp.float32
        )
        return ((key_total, value_total), query_grad)

    starts = jnp.arange(block_count // QG) * QG
    empty = jnp.zeros((block_count, BLK * HD), jnp.float32)
    (key_total, value_total), query_grad = lax.scan(one_group, (empty, empty), starts)
    query_grad = query_grad.reshape(block_count * BLK, HD)
    key_grad = (key_total * score_scale).astype(jnp.bfloat16).reshape(block_count * BLK, HD)
    value_grad = value_total.astype(jnp.bfloat16).reshape(block_count * BLK, HD)
    return (query_grad, key_grad, value_grad)


def body(queries, keys, values, attn_out, out_grad, random_blocks, global_blocks, radius):
    head_query, head_key, head_value, head_output, head_grad = (
        lax.all_to_all(queries, "ctx", split_axis=2, concat_axis=1, tiled=True),
        lax.all_to_all(keys, "ctx", split_axis=2, concat_axis=1, tiled=True),
        lax.all_to_all(values, "ctx", split_axis=2, concat_axis=1, tiled=True),
        lax.all_to_all(attn_out, "ctx", split_axis=2, concat_axis=1, tiled=True),
        lax.all_to_all(out_grad, "ctx", split_axis=2, concat_axis=1, tiled=True),
    )
    length = head_query.shape[1]
    local_heads = head_query.shape[2] // HD
    correction = lane_sums(
        head_output.reshape(1, length, local_heads, HD),
        head_grad.reshape(1, length, local_heads, HD),
    )
    local_heads = head_query.shape[2] // HD
    columns = slice(0, HD)
    query_grad, key_grad, value_grad = head_grads(
        head_query[0, :, columns],
        head_key[0, :, columns],
        head_value[0, :, columns],
        head_grad[0, :, columns],
        correction[0, :, 0],
        random_blocks[0, 0],
        global_blocks[0],
        radius[0, 0],
    )
    gradients = jnp.stack([query_grad, key_grad, value_grad], axis=0)[:, None]
    returned = lax.all_to_all(gradients, "ctx", split_axis=2, concat_axis=3, tiled=True)
    arrived = passed_along(returned, "pipe", -1)
    return (arrived[0], arrived[1], arrived[2])


def solution(mesh):
    return jax.shard_map(
        body,
        mesh=mesh,
        in_specs=(
            P("pipe", "ctx", None),
            P("pipe", "ctx", None),
            P("pipe", "ctx", None),
            P("pipe", "ctx", None),
            P("pipe", "ctx", None),
            P("pipe", "ctx", None, None),
            P("pipe", None),
            P("pipe", "ctx"),
        ),
        out_specs=(P("pipe", "ctx", None), P("pipe", "ctx", None), P("pipe", "ctx", None)),
        check_vma=False,
    )
```

profile of v0, /device:TPU:1, one launch (start us, length us, event | category | flops | bytes accessed | tf_op | source)
XLA Modules:
  0.0 691.4 jit_solution(3119696237251115099)
XLA Ops:
  0.6 5.0 copy.91
  6.2 22.3 %reduce = bf16[4096,128]{1,0:T(8,128)(2,1)S(1)} reduce(bf16[4096,1,128]{2,1,0:T(2,128)(2,1)S(1)} %bitcast.108, bf16[]{:T(256)} %broadcast.74), dimensions={1}, to_apply=%bitcast.48.reduce_sub_computation | reduce | bytes 2097154
  29.6 11.9 %all-to-all-start = ((bf16[32,2,8192]{2,1,0:T(2,128)(2,1)}), bf16[32,2,8192]{2,1,0:T(2,128)(2,1)S(1)}, u32[]{:S(2)}, u32[]{:S(2)}) async-start(bf16[32,2,8192]{2,1,0:T(2,128)(2,1)} %reshape.110), calls=%async_computation | async-start | bytes 2097152 | tf_op jit(solution)/shard_map/all_to_all | solution.py:122
  41.5 5.0 copy.93
  46.5 23.3 %reduce.1 = bf16[4096,128]{1,0:T(8,128)(2,1)} reduce(bf16[4096,1,128]{2,1,0:T(2,128)(2,1)S(1)} %bitcast.111, bf16[]{:T(256)} %broadcast.74), dimensions={1}, to_apply=%bitcast.50.reduce_sub_computation | reduce | bytes 2097154
  72.0 9.8 %all-to-all-start.1 = ((bf16[32,2,8192]{2,1,0:T(2,128)(2,1)}), bf16[32,2,8192]{2,1,0:T(2,128)(2,1)}, u32[]{:S(2)}, u32[]{:S(2)}) async-start(bf16[32,2,8192]{2,1,0:T(2,128)(2,1)} %reshape.112), calls=%async_computation.1 | async-start | bytes 2097152 | tf_op jit(solution)/shard_map/all_to_all | solution.py:123
  81.8 5.0 copy.97
  86.8 23.3 %reduce.3 = bf16[4096,128]{1,0:T(8,128)(2,1)} reduce(bf16[4096,1,128]{2,1,0:T(2,128)(2,1)S(1)} %bitcast.112, bf16[]{:T(256)} %broadcast.74), dimensions={1}, to_apply=%bitcast.54.reduce_sub_computation | reduce | bytes 2097154
  112.2 9.5 %all-to-all-start.3 = ((bf16[32,2,8192]{2,1,0:T(2,128)(2,1)}), bf16[32,2,8192]{2,1,0:T(2,128)(2,1)}, u32[]{:S(2)}, u32[]{:S(2)}) async-start(bf16[32,2,8192]{2,1,0:T(2,128)(2,1)} %reshape.116), calls=%async_computation.3 | async-start | bytes 2097152 | tf_op jit(solution)/shard_map/all_to_all | solution.py:124
  121.7 5.0 copy.99
  126.8 23.3 %reduce.4 = bf16[4096,128]{1,0:T(8,128)(2,1)} reduce(bf16[4096,1,128]{2,1,0:T(2,128)(2,1)S(1)} %bitcast.113, bf16[]{:T(256)} %broadcast.74), dimensions={1}, to_apply=%bitcast.56.reduce_sub_computation | reduce | bytes 2097154
  152.2 9.5 %all-to-all-start.4 = ((bf16[32,2,8192]{2,1,0:T(2,128)(2,1)}), bf16[32,2,8192]{2,1,0:T(2,128)(2,1)}, u32[]{:S(2)}, u32[]{:S(2)}) async-start(bf16[32,2,8192]{2,1,0:T(2,128)(2,1)} %reshape.118), calls=%async_computation.4 | async-start | bytes 2097152 | tf_op jit(solution)/shard_map/all_to_all | solution.py:125
  162.4 5.0 copy.95
  167.4 23.3 %reduce.2 = bf16[4096,128]{1,0:T(8,128)(2,1)} reduce(bf16[4096,1,128]{2,1,0:T(2,128)(2,1)S(1)} %bitcast.109, bf16[]{:T(256)} %broadcast.74), dimensions={1}, to_apply=%bitcast.52.reduce_sub_computation | reduce | bytes 2097154
  193.1 9.5 %all-to-all-start.2 = ((bf16[32,2,8192]{2,1,0:T(2,128)(2,1)}), bf16[32,2,8192]{2,1,0:T(2,128)(2,1)}, u32[]{:S(2)}, u32[]{:S(2)}) async-start(bf16[32,2,8192]{2,1,0:T(2,128)(2,1)} %reshape.114), calls=%async_computation.2 | async-start | bytes 2097152 | tf_op jit(solution)/shard_map/all_to_all | solution.py:126
  234.2 6.2 fusion.25
  240.4 274.9 %while.15 = (s32[]{:T(128)}, f32[64,8192]{1,0:T(8,128)}, f32[64,8192]{1,0:T(8,128)}, bf16[8,8,64,128]{3,2,1,0:T(8,128)(2,1)}, s32[8]{0:T(128)S(1)}, /*index=5*/s...) while((s32[]{:T(128)}, f32[64,8192]{1,0:T(8,128)}, ...), condition=%wide.region_5.6_spmd.clone, body=%wide.region_2.5_spmd.clone.sunk | while | flops 1431909376 | bytes 54307064 | solution.py:113
  396.6 4.4 convolution_add_fusion.5
  431.3 4.4 convolution_add_fusion.5
  466.1 4.4 convolution_add_fusion.5
  521.4 20.0 %copy.103 = bf16[3,1,4096,128]{3,0,1,2:T(4,128)(2,1)S(1)} copy(bf16[3,1,4096,128]{3,2,0,1:T(8,128)(2,1)S(1)} %maximum_bitcast_fusion) | data formatting | bytes 6291456 | tf_op jit(solution)/shard_map/broadcast_in_dim | solution.py:146
  541.4 98.1 %all_to_all.87 = bf16[3,1,4096,128]{3,0,1,2:T(4,128)(2,1)S(1)} all-to-all(bf16[3,1,4096,128]{3,0,1,2:T(4,128)(2,1)S(1)} %copy.103), channel_id=1, replica_groups=mesh['pipe'=8,'ctx'=32] {'ctx'}, dimensions={2} | all-to-all | bytes 6291456 | tf_op jit(solution)/shard_map/all_to_all | solution.py:147
  642.8 7.9 %collective-permute-start = (bf16[3,1,128,4096]{2,3,0,1:T(8,128)(2,1)}, bf16[3,1,128,4096]{2,3,0,1:T(8,128)(2,1)S(1)}, u32[]{:S(2)}, u32[]{:S(2)}) collective-permute-start(bf16[3,1,128,4096]{2,3,0,1:T(8,128)(2,1)} %bitcast.119), channel_id=1, source_target_pairs={{0,224},{32,0},{64,32},{96,64},{128,96},{160,128},{192,160},{224,1... | collective-permute-start | bytes 9437192 | tf_op jit(solution)/shard_map/ppermute | solution.py:17
  650.7 36.4 %collective-permute-done = bf16[3,1,128,4096]{2,3,0,1:T(8,128)(2,1)S(1)} collective-permute-done((bf16[3,1,128,4096]{2,3,0,1:T(8,128)(2,1)}, bf16[3,1,128,4096]{2,3,0,1:T(8,128)(2,1)S(1)}, u32[]{:S(2)}, u32[]{:S(2)}) %collective-permute-start) | collective-permute-done | bytes 3145760 | tf_op jit(solution)/shard_map/ppermute | solution.py:17
  (247 shorter events, 300.8 us)
Async XLA Ops:
  29.6 42.3 %all-to-all-start = ((bf16[32,2,8192]{2,1,0:T(2,128)(2,1)}), bf16[32,2,8192]{2,1,0:T(2,128)(2,1)S(1)}, u32[]{:S(2)}, u32[]{:S(2)}) async-start(bf16[32,2,8192]{2,1,0:T(2,128)(2,1)} %reshape.110), calls=%async_computation | async-start | bytes 2097152 | tf_op jit(solution)/shard_map/all_to_all | solution.py:122
  72.0 40.3 %all-to-all-start.1 = ((bf16[32,2,8192]{2,1,0:T(2,128)(2,1)}), bf16[32,2,8192]{2,1,0:T(2,128)(2,1)}, u32[]{:S(2)}, u32[]{:S(2)}) async-start(bf16[32,2,8192]{2,1,0:T(2,128)(2,1)} %reshape.112), calls=%async_computation.1 | async-start | bytes 2097152 | tf_op jit(solution)/shard_map/all_to_all | solution.py:123
  112.2 40.0 %all-to-all-start.3 = ((bf16[32,2,8192]{2,1,0:T(2,128)(2,1)}), bf16[32,2,8192]{2,1,0:T(2,128)(2,1)}, u32[]{:S(2)}, u32[]{:S(2)}) async-start(bf16[32,2,8192]{2,1,0:T(2,128)(2,1)} %reshape.116), calls=%async_computation.3 | async-start | bytes 2097152 | tf_op jit(solution)/shard_map/all_to_all | solution.py:124
  150.1 12.3 %copy-start.4 = (s32[1,1,64,3]{2,1,3,0:T(1,128)S(1)}, s32[1,1,64,3]{2,1,3,0:T(1,128)}, u32[]{:S(2)}) copy-start(s32[1,1,64,3]{2,1,3,0:T(1,128)} %param.15) | copy-start | bytes 2308
  152.2 40.8 %all-to-all-start.4 = ((bf16[32,2,8192]{2,1,0:T(2,128)(2,1)}), bf16[32,2,8192]{2,1,0:T(2,128)(2,1)}, u32[]{:S(2)}, u32[]{:S(2)}) async-start(bf16[32,2,8192]{2,1,0:T(2,128)(2,1)} %reshape.118), calls=%async_computation.4 | async-start | bytes 2097152 | tf_op jit(solution)/shard_map/all_to_all | solution.py:125
  167.4 25.6 %copy-start.5 = (s32[1,2]{1,0:T(1,128)S(1)}, s32[1,2]{1,0:T(1,128)}, u32[]{:S(2)}) copy-start(s32[1,2]{1,0:T(1,128)} %param.16) | copy-start | bytes 28
  193.1 34.7 %all-to-all-start.2 = ((bf16[32,2,8192]{2,1,0:T(2,128)(2,1)}), bf16[32,2,8192]{2,1,0:T(2,128)(2,1)}, u32[]{:S(2)}, u32[]{:S(2)}) async-start(bf16[32,2,8192]{2,1,0:T(2,128)(2,1)} %reshape.114), calls=%async_computation.2 | async-start | bytes 2097152 | tf_op jit(solution)/shard_map/all_to_all | solution.py:126
  232.2 2.0 copy-start.2
  250.2 1.5 copy-start.1
  281.8 1.5 copy-start.1
  316.5 1.5 copy-start.1
  351.2 1.5 copy-start.1
  386.0 1.5 copy-start.1
  420.7 1.5 copy-start.1
  455.4 1.5 copy-start.1
  490.2 1.5 copy-start.1
  515.3 3.2 copy-start
  518.6 1.2 copy-start.3
  642.8 44.3 %collective-permute-start = (bf16[3,1,128,4096]{2,3,0,1:T(8,128)(2,1)}, bf16[3,1,128,4096]{2,3,0,1:T(8,128)(2,1)S(1)}, u32[]{:S(2)}, u32[]{:S(2)}) collective-permute-start(bf16[3,1,128,4096]{2,3,0,1:T(8,128)(2,1)} %bitcast.119), channel_id=1, source_target_pairs={{0,224},{32,0},{64,32},{96,64},{128,96},{160,128},{192,160},{224,1... | collective-permute-start | bytes 9437192 | tf_op jit(solution)/shard_map/ppermute | solution.py:17
where the time goes:
time: 704 us; the launch traced here: 691 us
  local copies, waits for them, and re-layouts  184 us (26%)
  matrix products  162 us (23%)
  other arithmetic  135 us (19%)
  blocking collectives  98.1 us (14%)
  starting transfers between devices  58 us (8%)
  waiting for transfers between devices  36.4 us (5%)
  loops' own time  16.2 us (2%)
    unnamed x7, other arithmetic  116 us
    all_to_all x1, blocking collectives, body(): lax.all_to_all(gradients, 'ctx', split_axis=2, concat_axis=3, tiled=True)  98.1 us
    unnamed x36, local copies, waits for them, and re-layouts  59.7 us
    ppermute x1, waiting for transfers between devices, passed_along(): return lax.ppermute(value, axis, pairs)  36.4 us
    dot_general x8, matrix products, one_group(): jnp.dot(placing, value_part, precision=lax.Precision.HIGHEST, preferred_e...  34 us
    dot_general x8, matrix products, one_group(): jnp.dot(placing, key_part, precision=lax.Precision.HIGHEST, preferred_ele...  33.5 us
    dot_general x8, matrix products, one_group(): jnp.einsum('bij,bid->bjd', attention_low, group_grad, preferred_element_t...  31.2 us
    gather x8, local copies, waits for them, and re-layouts, one_group(): value_tiles = value_blocks[group_index].reshape(QG, KB * BLK, HD)  24.8 us
  transfers between devices with their start and end apart: 6, of which 1 were waited for; matrix products, arithmetic and copies ran while one was open for 21% of the time, Pallas kernels for 0%

commit v1 on v0

--- a/solution.py
+++ b/solution.py
@@ -144,7 +144,10 @@
         radius[0, 0],
     )
     gradients = jnp.stack([query_grad, key_grad, value_grad], axis=0)[:, None]
-    returned = lax.all_to_all(gradients, "ctx", split_axis=2, concat_axis=3, tiled=True)
+    returned = jnp.concatenate(
+        lax.all_to_all(jnp.stack(jnp.split(gradients, lax.axis_size("ctx"), axis=2)), "ctx", 0, 0),
+        axis=3,
+    )
     arrived = passed_along(returned, "pipe", -1)
     return (arrived[0], arrived[1], arrived[2])
 

time: 704 us -> 665 us (0.945)
  blocking collectives: 98.1 us -> 75.6 us
  local copies, waits for them, and re-layouts: 184 us -> 163 us
    all_to_all x1, blocking collectives: 98.1 us -> 75.6 us  [body(): lax.all_to_all(jnp.stack(jnp.split(gradients, lax.axis_size('ctx'), axis=...]
    broadcast_in_dim x1 -> x0, local copies, waits for them, and re-layouts: 20 us -> none  [body(): gradients = jnp.stack([query_grad, key_grad, value_grad], axis=0)[:, None]]
    unnamed x36 -> x65, local copies, waits for them, and re-layouts: 59.7 us -> 59.4 us
  transfers between devices with their start and end apart: 6 -> 6, of which waited for: 1 -> 1; matrix products, arithmetic and copies ran while one was open for 21% -> 23% of each run, Pallas kernels for 0% -> 0%
where the time goes in v1:
time: 665 us; the launch traced here: 653 us
  matrix products  166 us (25%)
  local copies, waits for them, and re-layouts  163 us (25%)
  other arithmetic  135 us (20%)
  blocking collectives  75.6 us (11%)
  starting transfers between devices  58 us (9%)
  waiting for transfers between devices  36.4 us (5%)
  loops' own time  16.1 us (2%)
    unnamed x7, other arithmetic  116 us
    all_to_all x1, blocking collectives, body(): lax.all_to_all(jnp.stack(jnp.split(gradients, lax.axis_size('ctx'), axis=...  75.6 us
    unnamed x65, local copies, waits for them, and re-layouts  59.4 us
    ppermute x1, waiting for transfers between devices, passed_along(): return lax.ppermute(value, axis, pairs)  36.3 us
    dot_general x8, matrix products, one_group(): jnp.dot(placing, value_part, precision=lax.Precision.HIGHEST, preferred_e...  34 us
    dot_general x8, matrix products, one_group(): jnp.dot(placing, key_part, precision=lax.Precision.HIGHEST, preferred_ele...  33.5 us
    dot_general x8, matrix products, one_group(): jnp.einsum('bij,bid->bjd', attention_low, group_grad, preferred_element_t...  31.2 us
    gather x8, local copies, waits for them, and re-layouts, one_group(): value_tiles = value_blocks[group_index].reshape(QG, KB * BLK, HD)  24.8 us
  transfers between devices with their start and end apart: 6, of which 1 were waited for; matrix products, arithmetic and copies ran while one was open for 23% of the time, Pallas kernels for 0%

profile of v1, /device:TPU:1, one launch (start us, length us, event | category | flops | bytes accessed | tf_op | source)
XLA Modules:
  0.0 652.8 jit_solution(6998634171446921796)
XLA Ops:
  0.6 5.0 copy.117
  6.2 22.3 %reduce = bf16[4096,128]{1,0:T(8,128)(2,1)S(1)} reduce(bf16[4096,1,128]{2,1,0:T(2,128)(2,1)S(1)} %bitcast.234, bf16[]{:T(256)} %broadcast.74), dimensions={1}, to_apply=%bitcast.174.reduce_sub_computation | reduce | bytes 2097154
  29.6 11.9 %all-to-all-start = ((bf16[32,2,8192]{2,1,0:T(2,128)(2,1)}), bf16[32,2,8192]{2,1,0:T(2,128)(2,1)S(1)}, u32[]{:S(2)}, u32[]{:S(2)}) async-start(bf16[32,2,8192]{2,1,0:T(2,128)(2,1)} %reshape.118), calls=%async_computation | async-start | bytes 2097152 | tf_op jit(solution)/shard_map/all_to_all | solution.py:122
  41.5 5.0 copy.119
  46.5 23.3 %reduce.1 = bf16[4096,128]{1,0:T(8,128)(2,1)} reduce(bf16[4096,1,128]{2,1,0:T(2,128)(2,1)S(1)} %bitcast.237, bf16[]{:T(256)} %broadcast.74), dimensions={1}, to_apply=%bitcast.176.reduce_sub_computation | reduce | bytes 2097154
  72.0 9.8 %all-to-all-start.1 = ((bf16[32,2,8192]{2,1,0:T(2,128)(2,1)}), bf16[32,2,8192]{2,1,0:T(2,128)(2,1)}, u32[]{:S(2)}, u32[]{:S(2)}) async-start(bf16[32,2,8192]{2,1,0:T(2,128)(2,1)} %reshape.120), calls=%async_computation.1 | async-start | bytes 2097152 | tf_op jit(solution)/shard_map/all_to_all | solution.py:123
  81.8 5.0 copy.123
  86.8 23.3 %reduce.3 = bf16[4096,128]{1,0:T(8,128)(2,1)} reduce(bf16[4096,1,128]{2,1,0:T(2,128)(2,1)S(1)} %bitcast.238, bf16[]{:T(256)} %broadcast.74), dimensions={1}, to_apply=%bitcast.180.reduce_sub_computation | reduce | bytes 2097154
  112.2 9.5 %all-to-all-start.3 = ((bf16[32,2,8192]{2,1,0:T(2,128)(2,1)}), bf16[32,2,8192]{2,1,0:T(2,128)(2,1)}, u32[]{:S(2)}, u32[]{:S(2)}) async-start(bf16[32,2,8192]{2,1,0:T(2,128)(2,1)} %reshape.124), calls=%async_computation.3 | async-start | bytes 2097152 | tf_op jit(solution)/shard_map/all_to_all | solution.py:124
  121.7 5.0 copy.125
  126.8 23.3 %reduce.4 = bf16[4096,128]{1,0:T(8,128)(2,1)} reduce(bf16[4096,1,128]{2,1,0:T(2,128)(2,1)S(1)} %bitcast.239, bf16[]{:T(256)} %broadcast.74), dimensions={1}, to_apply=%bitcast.182.reduce_sub_computation | reduce | bytes 2097154
  152.2 9.5 %all-to-all-start.4 = ((bf16[32,2,8192]{2,1,0:T(2,128)(2,1)}), bf16[32,2,8192]{2,1,0:T(2,128)(2,1)}, u32[]{:S(2)}, u32[]{:S(2)}) async-start(bf16[32,2,8192]{2,1,0:T(2,128)(2,1)} %reshape.126), calls=%async_computation.4 | async-start | bytes 2097152 | tf_op jit(solution)/shard_map/all_to_all | solution.py:125
  162.4 5.0 copy.121
  167.4 23.3 %reduce.2 = bf16[4096,128]{1,0:T(8,128)(2,1)} reduce(bf16[4096,1,128]{2,1,0:T(2,128)(2,1)S(1)} %bitcast.235, bf16[]{:T(256)} %broadcast.74), dimensions={1}, to_apply=%bitcast.178.reduce_sub_computation | reduce | bytes 2097154
  193.1 9.5 %all-to-all-start.2 = ((bf16[32,2,8192]{2,1,0:T(2,128)(2,1)}), bf16[32,2,8192]{2,1,0:T(2,128)(2,1)}, u32[]{:S(2)}, u32[]{:S(2)}) async-start(bf16[32,2,8192]{2,1,0:T(2,128)(2,1)} %reshape.122), calls=%async_computation.2 | async-start | bytes 2097152 | tf_op jit(solution)/shard_map/all_to_all | solution.py:126
  234.2 6.2 fusion.25
  240.4 278.8 %while.15 = (s32[]{:T(128)}, f32[64,8192]{1,0:T(8,128)}, f32[64,8192]{1,0:T(8,128)}, bf16[8,8,64,128]{3,2,1,0:T(8,128)(2,1)}, s32[8]{0:T(128)S(1)}, /*index=5*/s...) while((s32[]{:T(128)}, f32[64,8192]{1,0:T(8,128)}, ...), condition=%wide.region_5.6_spmd.clone, body=%wide.region_2.5_spmd.clone.sunk | while | flops 1431909376 | bytes 49064156 | solution.py:113
  293.4 4.4 convolution_add_fusion.5
  328.6 4.4 convolution_add_fusion.5
  363.8 4.4 convolution_add_fusion.5
  399.1 4.4 convolution_add_fusion.5
  525.7 75.6 %all_to_all.74 = bf16[32,3,1,128,128]{4,3,1,2,0:T(8,128)(2,1)S(1)} all-to-all(bf16[32,3,1,128,128]{4,3,1,2,0:T(8,128)(2,1)S(1)} %fusion.28), channel_id=1, replica_groups=mesh['pipe'=8,'ctx'=32] {'ctx'}, dimensions={0} | all-to-all | bytes 6291456 | tf_op jit(solution)/shard_map/all_to_all | solution.py:148
  604.2 7.9 %collective-permute-start = (bf16[3,1,128,4096]{2,3,0,1:T(8,128)(2,1)}, bf16[3,1,128,4096]{2,3,0,1:T(8,128)(2,1)S(1)}, u32[]{:S(2)}, u32[]{:S(2)}) collective-permute-start(bf16[3,1,128,4096]{2,3,0,1:T(8,128)(2,1)} %bitcast.245), channel_id=1, source_target_pairs={{0,224},{32,0},{64,32},{96,64},{128,96},{160,128},{192,160},{224,1... | collective-permute-start | bytes 9437192 | tf_op jit(solution)/shard_map/ppermute | solution.py:17
  612.1 36.3 %collective-permute-done = bf16[3,1,128,4096]{2,3,0,1:T(8,128)(2,1)S(1)} collective-permute-done((bf16[3,1,128,4096]{2,3,0,1:T(8,128)(2,1)}, bf16[3,1,128,4096]{2,3,0,1:T(8,128)(2,1)S(1)}, u32[]{:S(2)}, u32[]{:S(2)}) %collective-permute-start) | collective-permute-done | bytes 3145760 | tf_op jit(solution)/shard_map/ppermute | solution.py:17
  (259 shorter events, 300.0 us)
Async XLA Ops:
  29.6 42.3 %all-to-all-start = ((bf16[32,2,8192]{2,1,0:T(2,128)(2,1)}), bf16[32,2,8192]{2,1,0:T(2,128)(2,1)S(1)}, u32[]{:S(2)}, u32[]{:S(2)}) async-start(bf16[32,2,8192]{2,1,0:T(2,128)(2,1)} %reshape.118), calls=%async_computation | async-start | bytes 2097152 | tf_op jit(solution)/shard_map/all_to_all | solution.py:122
  72.0 40.3 %all-to-all-start.1 = ((bf16[32,2,8192]{2,1,0:T(2,128)(2,1)}), bf16[32,2,8192]{2,1,0:T(2,128)(2,1)}, u32[]{:S(2)}, u32[]{:S(2)}) async-start(bf16[32,2,8192]{2,1,0:T(2,128)(2,1)} %reshape.120), calls=%async_computation.1 | async-start | bytes 2097152 | tf_op jit(solution)/shard_map/all_to_all | solution.py:123
  112.2 40.0 %all-to-all-start.3 = ((bf16[32,2,8192]{2,1,0:T(2,128)(2,1)}), bf16[32,2,8192]{2,1,0:T(2,128)(2,1)}, u32[]{:S(2)}, u32[]{:S(2)}) async-start(bf16[32,2,8192]{2,1,0:T(2,128)(2,1)} %reshape.124), calls=%async_computation.3 | async-start | bytes 2097152 | tf_op jit(solution)/shard_map/all_to_all | solution.py:124
  126.8 35.6 %copy-start.2 = (s32[1,1,64,3]{2,1,3,0:T(1,128)S(1)}, s32[1,1,64,3]{2,1,3,0:T(1,128)}, u32[]{:S(2)}) copy-start(s32[1,1,64,3]{2,1,3,0:T(1,128)} %param.15) | copy-start | bytes 2308
  152.2 40.8 %all-to-all-start.4 = ((bf16[32,2,8192]{2,1,0:T(2,128)(2,1)}), bf16[32,2,8192]{2,1,0:T(2,128)(2,1)}, u32[]{:S(2)}, u32[]{:S(2)}) async-start(bf16[32,2,8192]{2,1,0:T(2,128)(2,1)} %reshape.126), calls=%async_computation.4 | async-start | bytes 2097152 | tf_op jit(solution)/shard_map/all_to_all | solution.py:125
  167.4 25.6 %copy-start.3 = (s32[1,2]{1,0:T(1,128)S(1)}, s32[1,2]{1,0:T(1,128)}, u32[]{:S(2)}) copy-start(s32[1,2]{1,0:T(1,128)} %param.16) | copy-start | bytes 28
  193.1 34.7 %all-to-all-start.2 = ((bf16[32,2,8192]{2,1,0:T(2,128)(2,1)}), bf16[32,2,8192]{2,1,0:T(2,128)(2,1)}, u32[]{:S(2)}, u32[]{:S(2)}) async-start(bf16[32,2,8192]{2,1,0:T(2,128)(2,1)} %reshape.122), calls=%async_computation.2 | async-start | bytes 2097152 | tf_op jit(solution)/shard_map/all_to_all | solution.py:126
  232.2 2.0 copy-start.1
  519.2 3.2 copy-start
  604.2 44.2 %collective-permute-start = (bf16[3,1,128,4096]{2,3,0,1:T(8,128)(2,1)}, bf16[3,1,128,4096]{2,3,0,1:T(8,128)(2,1)S(1)}, u32[]{:S(2)}, u32[]{:S(2)}) collective-permute-start(bf16[3,1,128,4096]{2,3,0,1:T(8,128)(2,1)} %bitcast.245), channel_id=1, source_target_pairs={{0,224},{32,0},{64,32},{96,64},{128,96},{160,128},{192,160},{224,1... | collective-permute-start | bytes 9437192 | tf_op jit(solution)/shard_map/ppermute | solution.py:17
